TPU v7x, 256 devices: a whole 4x4x8 slice. The times are simulated.
256 devices in a mesh: dp: 32 (over y, z), expert: 8 (over x, core).
Axes of the slice: x: 4, y: 4, z: 8, core: 2. Of those that a mesh axis runs over, the one named last changes fastest.
Arguments:
- master: float32 [8, 4096, 1536], P('expert', 'dp'), may hold values from -0.109375 to 0.109375
- moment_one: float32 [8, 4096, 1536], P('expert', 'dp'), may hold values from -1.5 to 1.5
- moment_two: float32 [8, 4096, 1536], P('expert', 'dp'), may hold values from 0.0001 to 0.003
- saved_rows: bfloat16 [8, 12288, 1536], P('expert', 'dp'), may hold values from -6 to 6
- saved_grads: bfloat16 [8, 12288, 4096], P('expert', 'dp'), may hold values from -0.109375 to 0.109375
- slot_rows: bfloat16 [32768, 2, 1536], P(('dp', 'expert')), may hold values from -6 to 6
- routes: int32 [32768, 2], P(('dp', 'expert')), may hold values from 0 to 7, all different within a row; in each aligned block of 128 rows (0 to 127, 128 to 255, ...) at most 40 rows name the same one
- gates: float32 [32768, 2], P(('dp', 'expert')), may hold values from 0.1 to 1
Outputs:
- master_new: float32 [8, 4096, 1536], P('expert', 'dp')
- moment_one_new: float32 [8, 4096, 1536], P('expert', 'dp')
- moment_two_new: float32 [8, 4096, 1536], P('expert', 'dp')
- mixed: bfloat16 [32768, 4096], P(('dp', 'expert'))
Inputs may be any that keep to these rules, and one draw needn't show every extreme that they name: `routes`: each token names 2 different experts. Among the 128 tokens of one device (aligned blocks of rows in device order, dp slowest) at most 40 name the same expert, and in some device's block exactly 40 do.
All inputs are finite; a program needn't handle non-finite values.
Results may differ from a plain program's by a relative error of at most 0.034.
Values may be sent and summed in bfloat16 or wider, within the bound.
No kernel may reach another device: no remote copies, remote signals or barrier semaphores. Data moves between devices by JAX's collectives and lax.ppermute only.
A program may use at most 128 MiB of HBM per device.

v0:
```python
import jax
import jax.numpy as jnp
from jax import lax
from jax.sharding import PartitionSpec as P

beta_one = 0.9
beta_two = 0.999
learn_rate = 0.002
tiny_eps = 1e-08
steps_done = 100.0


def adam_update(master, moment_one, moment_two, grad):
    m_new = beta_one * moment_one + (1.0 - beta_one) * grad
    v_new = beta_two * moment_two + (1.0 - beta_two) * grad * grad
    fix_one = 1.0 - beta_one**steps_done
    fix_two = 1.0 - beta_two**steps_done
    step_size = m_new / fix_one / (jnp.sqrt(v_new / fix_two) + tiny_eps)
    return (master - learn_rate * step_size, m_new, v_new)


def slot_places(routes, experts):
    flat = routes.reshape(-1)
    onehot = (flat[:, None] == jnp.arange(experts, dtype=jnp.int32)[None, :]).astype(jnp.int32)
    place = jnp.sum((jnp.cumsum(onehot, axis=0) - onehot) * onehot, axis=1)
    return (flat, place)


def send_back(results):
    return lax.all_to_all(results, "expert", split_axis=0, concat_axis=0, tiled=True)


def body(master, moment_one, moment_two, saved_rows, saved_grads, slot_rows, routes, gates):
    rows_here = saved_rows[0]
    grads_here = saved_grads[0]
    grad = lax.psum_scatter(
        lax.dot_general(
            grads_here, rows_here, (((0,), (0,)), ((), ())), preferred_element_type=jnp.float32
        ).astype(jnp.bfloat16),
        "dp",
        scatter_dimension=0,
        tiled=True,
    ).astype(jnp.float32)
    master_new, m_new, v_new = adam_update(master[0], moment_one[0], moment_two[0], grad)
    weights_shard = master_new.astype(jnp.bfloat16)
    experts = lax.axis_size("expert")
    tok_count, top_count, width = slot_rows.shape
    capacity = tok_count * top_count * 5 // (4 * experts)
    flat, place = slot_places(routes, experts)
    outgoing = (
        jnp.zeros((experts, capacity, width), jnp.bfloat16)
        .at[flat, place]
        .set(slot_rows.reshape(-1, width))
    )
    weights = lax.all_gather(weights_shard, "dp", axis=0, tiled=True)
    out_width = weights.shape[0]
    received = lax.all_to_all(outgoing, "expert", split_axis=0, concat_axis=0, tiled=True)
    sources, count, _ = received.shape
    product = lax.dot_general(
        received.reshape(-1, width),
        weights,
        (((1,), (1,)), ((), ())),
        preferred_element_type=jnp.float32,
    )
    returned = send_back(product.astype(jnp.bfloat16).reshape(sources, count, out_width))
    out_width = returned.shape[2]
    picked = returned[flat, place].astype(jnp.float32).reshape(tok_count, top_count, out_width)
    mixed = jnp.sum(picked * gates[:, :, None], axis=1).astype(jnp.bfloat16)
    return (master_new[None], m_new[None], v_new[None], mixed)


def solution(mesh):
    placed = (
        P("expert", "dp", None),
        P("expert", "dp", None),
        P("expert", "dp", None),
        P("expert", "dp", None),
        P("expert", "dp", None),
        P(("dp", "expert"), None, None),
        P(("dp", "expert"), None),
        P(("dp", "expert"), None),
    )
    return jax.shard_map(
        body,
        mesh=mesh,
        in_specs=placed,
        out_specs=(
            P("expert", "dp", None),
            P("expert", "dp", None),
            P("expert", "dp", None),
            P(("dp", "expert"), None),
        ),
        check_vma=False,
    )
```

profile of v0, /device:TPU:1, one launch (start us, length us, event | category | flops | bytes accessed | tf_op | source)
XLA Modules:
  0.0 461.5 jit_solution(4875685492731966594)
XLA Ops:
  7.2 0.0 copy-start
  7.2 0.0 reduce-scatter.2.cloned.1.call-start
  7.2 1.8 copy-done
  9.1 10.9 %convolution_convert_fusion = bf16[4096,1536]{1,0:T(8,128)(2,1)} fusion(bf16[1,384,4096]{2,1,0:T(8,128)(2,1)S(1)} %copy-done, bf16[1,384,1536]{2,1,0:T(8,128)(2,1)} %param.11), kind=kOutput, calls=%fused_computation.2 | convolution fusion | flops 4838129664 | bytes 16908288 | tf_op jit(solution)/shard_map/dot_general | solution.py:37
  19.9 0.0 reduce-scatter.2.cloned.1.call-update
  20.0 0.0 copy-start.1
  20.0 0.0 all-gather.2.cloned.1.call-start
  20.0 238.8 %reduce-scatter.2.cloned.1.call-done = bf16[128,1536]{1,0:T(8,128)(2,1)} async-done(((bf16[4096,1536]{1,0:T(8,128)(2,1)}), bf16[128,1536]{1,0:T(8,128)(2,1)}) %reduce-scatter.2.cloned.1.call-update) | async-done | bytes 393232 | tf_op jit(solution)/shard_map/reduce_scatter | solution.py:36
  258.8 3.8 fusion.10
  262.6 0.0 all-gather.2.cloned.1.call-update
  262.6 0.0 copy-done.1
  262.6 0.1 copy.13
  262.8 0.1 reshape.87
  262.9 0.1 eq.29
  263.0 0.1 eq.25
  263.2 0.6 reduce-window.6
  263.8 0.2 slice_reduce_fusion
  264.0 3.0 reshape.101
  267.0 0.1 fusion.7
  267.1 1.0 broadcast_in_dim.21
  268.1 42.2 %scatter_fusion = bf16[8,40,1536]{2,1,0:T(8,128)(2,1)} fusion(bf16[8,40,1536]{2,1,0:T(8,128)(2,1)} %broadcast_in_dim.21, s32[256]{0:T(256)S(1)} %bitcast.44, bf16[256,1536]{1,0:T(8,128)(2,1)} %reshape.101), kind=kCustom, calls=%fused_computation.1 | custom fusion | bytes 2361344 | tf_op jit(solution)/shard_map/scatter | solution.py:53
  310.3 23.0 %all_to_all.10 = bf16[8,40,1536]{2,1,0:T(8,128)(2,1)} all-to-all(bf16[8,40,1536]{2,1,0:T(8,128)(2,1)} %scatter_fusion), channel_id=1, replica_groups=mesh['dp'=32,'expert'=8] {'expert'}, dimensions={0} | all-to-all | bytes 1966080 | tf_op jit(solution)/shard_map/all_to_all | solution.py:57
  333.3 50.5 %all-gather.2.cloned.1.call-done = bf16[4096,1536]{1,0:T(8,128)(2,1)} async-done(((bf16[128,1536]{1,0:T(8,128)(2,1)}), bf16[4096,1536]{1,0:T(8,128)(2,1)}) %all-gather.2.cloned.1.call-update) | async-done | bytes 12582928 | tf_op jit(solution)/shard_map/all_gather | solution.py:55
  383.9 10.6 %convolution_convert_fusion.1 = bf16[320,4096]{1,0:T(8,128)(2,1)} fusion(bf16[320,1536]{1,0:T(8,128)(2,1)} %bitcast.46, bf16[4096,1536]{1,0:T(8,128)(2,1)} %all-gather.2.cloned.1.call-done), kind=kOutput, calls=%fused_computation.3 | convolution fusion | flops 4027842560 | bytes 16187392 | tf_op jit(solution)/shard_map/dot_general | solution.py:59
  394.5 0.0 copy-start.2
  394.5 5.8 %all-to-all-start.1 = ((bf16[8,40,4096]{2,1,0:T(8,128)(2,1)}), bf16[8,40,4096]{2,1,0:T(8,128)(2,1)}, u32[]{:S(2)}, u32[]{:S(2)}) async-start(bf16[8,40,4096]{2,1,0:T(8,128)(2,1)} %bitcast.45), calls=%async_computation.2 | async-start | bytes 5242880 | tf_op jit(solution)/shard_map/all_to_all | solution.py:30
  400.3 0.0 copy-done.2
  400.3 0.1 copy.16
  400.4 31.8 %all-to-all-done.1 = bf16[8,40,4096]{2,1,0:T(8,128)(2,1)} async-done(((bf16[8,40,4096]{2,1,0:T(8,128)(2,1)}), bf16[8,40,4096]{2,1,0:T(8,128)(2,1)}, u32[]{:S(2)}, u32[]{:S(2)}) %all-to-all-start.1) | async-done | bytes 2621472 | tf_op jit(solution)/shard_map/all_to_all | solution.py:30
  432.2 7.3 %gather_fusion = bf16[256,4096]{1,0:T(8,128)(2,1)} fusion(bf16[8,40,4096]{2,1,0:T(8,128)(2,1)} %all-to-all-done.1, s32[256]{0:T(256)S(1)} %bitcast.43), kind=kCustom, calls=%fused_computation | custom fusion | bytes 4196352 | tf_op jit(solution)/shard_map/gather | solution.py:67
  439.6 5.4 %reshape.92 = f32[128,2,4096]{2,1,0:T(2,128)} reshape(bf16[256,4096]{1,0:T(8,128)(2,1)} %gather_fusion) | data formatting | bytes 6291456 | tf_op jit(solution)/shard_map/convert_element_type | solution.py:67
  445.0 9.6 %multiply_reduce_fusion = bf16[128,4096]{1,0:T(8,128)(2,1)} fusion(f32[128,2,4096]{2,1,0:T(2,128)} %reshape.92, f32[128,2]{1,0:T(8,128)S(1)} %copy.16), kind=kLoop, calls=%fused_computation.4 | loop fusion | flops 1572864 | bytes 5243904 | tf_op jit(solution)/shard_map/reduce_sum | solution.py:68
  (4 shorter events, 0.1 us)
Async XLA Ops:
  7.2 1.9 copy-start
  7.2 251.6 %reduce-scatter.2.cloned.1.call-start = ((), (), s32[]{:S(2)}) async-start(), calls=%async_computation.3 | async-start | bytes 12976128 | tf_op jit(solution)/shard_map/reduce_scatter | solution.py:36
  20.0 242.7 %copy-start.1 = (s32[128,2]{0,1:T(2,128)S(1)}, s32[128,2]{0,1:T(2,128)}, u32[]{:S(2)}) copy-start(s32[128,2]{0,1:T(2,128)} %param.14) | copy-start | bytes 3076
  20.0 363.9 %all-gather.2.cloned.1.call-start = ((), (), s32[]{:S(2)}) async-start(), calls=%async_computation.4 | async-start | bytes 12976128 | tf_op jit(solution)/shard_map/all_gather | solution.py:55
  394.5 5.8 %copy-start.2 = (f32[128,2]{0,1:T(2,128)S(1)}, f32[128,2]{0,1:T(2,128)}, u32[]{:S(2)}) copy-start(f32[128,2]{0,1:T(2,128)} %param.15) | copy-start | bytes 3076
  394.5 37.7 %all-to-all-start.1 = ((bf16[8,40,4096]{2,1,0:T(8,128)(2,1)}), bf16[8,40,4096]{2,1,0:T(8,128)(2,1)}, u32[]{:S(2)}, u32[]{:S(2)}) async-start(bf16[8,40,4096]{2,1,0:T(8,128)(2,1)} %bitcast.45), calls=%async_computation.2 | async-start | bytes 5242880 | tf_op jit(solution)/shard_map/all_to_all | solution.py:30
Sparse Core Ops, SparseCore 0:
  20.1 238.6 reduce-scatter.1
  262.7 121.0 all-gather.1
where the time goes:
time: 463 us; the launch traced here: 461 us
  waiting for transfers between devices  321 us (69%)
  local copies, waits for them, and re-layouts  61.6 us (13%)
  blocking collectives  23 us (5%)
  matrix products  21.5 us (5%)
  other arithmetic  14.2 us (3%)
  between operations  14.1 us (3%)
  starting transfers between devices  5.87 us (1%)
    reduce_scatter x1, waiting for transfers between devices, body(): lax.psum_scatter(lax.dot_general(grads_here, rows_here, (((0,), (0,)), ((...  239 us
    all_gather x1, waiting for transfers between devices, body(): weights = lax.all_gather(weights_shard, 'dp', axis=0, tiled=True)  50.5 us
    scatter x1, local copies, waits for them, and re-layouts, body(): outgoing = jnp.zeros((experts, capacity, width), jnp.bfloat16).at[flat, p...  42.2 us
    all_to_all x1, waiting for transfers between devices, send_back(): lax.all_to_all(results, 'expert', split_axis=0, concat_axis=0, tiled=True)  31.8 us
    all_to_all x1, blocking collectives, body(): lax.all_to_all(outgoing, 'expert', split_axis=0, concat_axis=0, tiled=True)  23 us
    dot_general x1, matrix products, body(): lax.dot_general(grads_here, rows_here, (((0,), (0,)), ((), ())), preferre...  10.9 us
    dot_general x1, matrix products, body(): lax.dot_general(received.reshape(-1, width), weights, (((1,), (1,)), ((),...  10.6 us
    reduce_sum x1, other arithmetic, body(): mixed = jnp.sum(picked * gates[:, :, None], axis=1).astype(jnp.bfloat16)  9.64 us
  transfers between devices with their start and end apart: 3, of which 3 were waited for; matrix products, arithmetic and copies ran while one was open for 10% of the time, Pallas kernels for 0%

commit v1 on v0

--- a/solution.py
+++ b/solution.py
@@ -8,6 +8,9 @@
 learn_rate = 0.002
 tiny_eps = 1e-08
 steps_done = 100.0
+apply_the_racks = lambda xx, d_out: jnp.concatenate(
+    lax.all_to_all(jnp.stack(lax.axis_size("dp") * [xx]), "dp", 0, 0), axis=d_out
+)
 
 
 def adam_update(master, moment_one, moment_two, grad):
@@ -52,7 +55,7 @@
         .at[flat, place]
         .set(slot_rows.reshape(-1, width))
     )
-    weights = lax.all_gather(weights_shard, "dp", axis=0, tiled=True)
+    weights = apply_the_racks(weights_shard, 0)
     out_width = weights.shape[0]
     received = lax.all_to_all(outgoing, "expert", split_axis=0, concat_axis=0, tiled=True)
     sources, count, _ = received.shape

time: 463 us -> 630 us (1.36)
  blocking collectives: 23 us -> 273 us
  waiting for transfers between devices: 321 us -> 216 us
  starting transfers between devices: 5.87 us -> 21 us
  local copies, waits for them, and re-layouts: 61.6 us -> 68 us
    all_to_all x1, blocking collectives: 23 us -> 273 us  [lax.all_to_all(jnp.stack(lax.axis_size('dp') * [xx]), 'dp', 0, 0)]
    reduce_scatter x1, waiting for transfers between devices: 239 us -> 184 us  [body(): lax.psum_scatter(lax.dot_general(grads_here, rows_here, (((0,), (0,)), ((...]
    all_gather x1 -> x0, waiting for transfers between devices: 50.5 us -> none  [body(): weights = lax.all_gather(weights_shard, 'dp', axis=0, tiled=True)]
    all_to_all x1, starting transfers between devices: 5.79 us -> 14.2 us  [send_back(): lax.all_to_all(results, 'expert', split_axis=0, concat_axis=0, tiled=True)]
    all_to_all x0 -> x1, starting transfers between devices: none -> 6.82 us  [body(): lax.all_to_all(outgoing, 'expert', split_axis=0, concat_axis=0, tiled=True)]
  transfers between devices with their start and end apart: 3 -> 3, of which waited for: 3 -> 2; matrix products, arithmetic and copies ran while one was open for 10% -> 8% of each run, Pallas kernels for 0% -> 0%
where the time goes in v1:
time: 630 us; the launch traced here: 628 us
  blocking collectives  273 us (43%)
  waiting for transfers between devices  216 us (34%)
  local copies, waits for them, and re-layouts  68 us (11%)
  matrix products  21.5 us (3%)
  starting transfers between devices  21 us (3%)
  between operations  14.1 us (2%)
  other arithmetic  13.8 us (2%)
    all_to_all x1, blocking collectives, lax.all_to_all(jnp.stack(lax.axis_size('dp') * [xx]), 'dp', 0, 0)  273 us
    reduce_scatter x1, waiting for transfers between devices, body(): lax.psum_scatter(lax.dot_general(grads_here, rows_here, (((0,), (0,)), ((...  184 us
    scatter x1, local copies, waits for them, and re-layouts, body(): outgoing = jnp.zeros((experts, capacity, width), jnp.bfloat16).at[flat, p...  42 us
    all_to_all x1, waiting for transfers between devices, send_back(): lax.all_to_all(results, 'expert', split_axis=0, concat_axis=0, tiled=True)  31.8 us
    all_to_all x1, starting transfers between devices, send_back(): lax.all_to_all(results, 'expert', split_axis=0, concat_axis=0, tiled=True)  14.2 us
  transfers between devices with their start and end apart: 3, of which 2 were waited for; matrix products, arithmetic and copies ran while one was open for 8% of the time, Pallas kernels for 0%

profile of v1, /device:TPU:1, one launch (start us, length us, event | category | flops | bytes accessed | tf_op | source)
XLA Modules:
  0.0 627.7 jit_solution(2390573944371875730)
XLA Ops:
  7.2 0.0 copy-start
  7.2 0.0 reduce-scatter.2.cloned.1.call-start
  7.2 1.8 copy-done
  9.1 10.9 %convolution_convert_fusion = bf16[4096,1536]{1,0:T(8,128)(2,1)} fusion(bf16[1,384,4096]{2,1,0:T(8,128)(2,1)S(1)} %copy-done, bf16[1,384,1536]{2,1,0:T(8,128)(2,1)} %param.11), kind=kOutput, calls=%fused_computation.2 | convolution fusion | flops 4838129664 | bytes 16908288 | tf_op jit(solution)/shard_map/dot_general | solution.py:40
  19.9 0.0 copy-start.1
  19.9 0.0 reduce-scatter.2.cloned.1.call-update
  20.0 0.7 copy-done.1
  20.6 0.1 copy.13
  20.7 0.1 reshape.92
  20.9 0.1 eq.29
  21.0 0.1 eq.25
  21.2 0.6 reduce-window.6
  21.8 0.2 slice_reduce_fusion
  22.0 3.0 reshape.107
  25.0 0.1 fusion.7
  25.1 1.0 broadcast_in_dim.21
  26.1 42.0 %scatter_fusion = bf16[8,40,1536]{2,1,0:T(8,128)(2,1)} fusion(bf16[8,40,1536]{2,1,0:T(8,128)(2,1)} %broadcast_in_dim.21, s32[256]{0:T(256)S(1)} %bitcast.45, bf16[256,1536]{1,0:T(8,128)(2,1)} %reshape.107), kind=kCustom, calls=%fused_computation.1 | custom fusion | bytes 2361344 | tf_op jit(solution)/shard_map/scatter | solution.py:56
  68.1 6.8 %all-to-all-start = ((bf16[8,40,1536]{2,1,0:T(8,128)(2,1)}), bf16[8,40,1536]{2,1,0:T(8,128)(2,1)}, u32[]{:S(2)}, u32[]{:S(2)}) async-start(bf16[8,40,1536]{2,1,0:T(8,128)(2,1)} %scatter_fusion), calls=%async_computation.1 | async-start | bytes 1966080 | tf_op jit(solution)/shard_map/all_to_all | solution.py:60
  74.9 184.2 %reduce-scatter.2.cloned.1.call-done = bf16[128,1536]{1,0:T(8,128)(2,1)} async-done(((bf16[4096,1536]{1,0:T(8,128)(2,1)}), bf16[128,1536]{1,0:T(8,128)(2,1)}) %reduce-scatter.2.cloned.1.call-update) | async-done | bytes 393232 | tf_op jit(solution)/shard_map/reduce_scatter | solution.py:39
  259.1 3.5 fusion.10
  262.6 0.0 all-to-all-done
  262.6 5.9 stack.2
  268.5 273.3 %all_to_all.15 = bf16[32,128,1536]{2,1,0:T(8,128)(2,1)} all-to-all(bf16[32,128,1536]{2,1,0:T(8,128)(2,1)} %stack.2), channel_id=1, replica_groups=mesh['dp'=32,'expert'=8] {'dp'}, dimensions={0} | all-to-all | bytes 25165824 | tf_op jit(solution)/shard_map/all_to_all | solution.py:12
  541.7 10.6 %convolution_convert_fusion.1 = bf16[320,4096]{1,0:T(8,128)(2,1)} fusion(bf16[320,1536]{1,0:T(8,128)(2,1)} %bitcast.12, bf16[4096,1536]{1,0:T(8,128)(2,1)} %bitcast.46), kind=kOutput, calls=%fused_computation.3 | convolution fusion | flops 4027842560 | bytes 16187392 | tf_op jit(solution)/shard_map/dot_general | solution.py:62
  552.4 0.0 copy-start.2
  552.4 14.2 %all-to-all-start.2 = ((bf16[8,40,4096]{2,1,0:T(8,128)(2,1)}), bf16[8,40,4096]{2,1,0:T(8,128)(2,1)}, u32[]{:S(2)}, u32[]{:S(2)}) async-start(bf16[8,40,4096]{2,1,0:T(8,128)(2,1)} %bitcast.47), calls=%async_computation.3 | async-start | bytes 5242880 | tf_op jit(solution)/shard_map/all_to_all | solution.py:33
  566.5 0.0 copy-done.2
  566.5 0.1 copy.16
  566.7 31.8 %all-to-all-done.2 = bf16[8,40,4096]{2,1,0:T(8,128)(2,1)} async-done(((bf16[8,40,4096]{2,1,0:T(8,128)(2,1)}), bf16[8,40,4096]{2,1,0:T(8,128)(2,1)}, u32[]{:S(2)}, u32[]{:S(2)}) %all-to-all-start.2) | async-done | bytes 2621472 | tf_op jit(solution)/shard_map/all_to_all | solution.py:33
  598.5 7.3 %gather_fusion = bf16[256,4096]{1,0:T(8,128)(2,1)} fusion(bf16[8,40,4096]{2,1,0:T(8,128)(2,1)} %all-to-all-done.2, s32[256]{0:T(256)S(1)} %bitcast.44), kind=kCustom, calls=%fused_computation | custom fusion | bytes 4196352 | tf_op jit(solution)/shard_map/gather | solution.py:70
  605.8 5.4 reshape.98
  611.3 9.6 %multiply_reduce_fusion = bf16[128,4096]{1,0:T(8,128)(2,1)} fusion(f32[128,2,4096]{2,1,0:T(2,128)} %reshape.98, f32[128,2]{1,0:T(8,128)S(1)} %copy.16), kind=kLoop, calls=%fused_computation.4 | loop fusion | flops 1572864 | bytes 5243904 | tf_op jit(solution)/shard_map/reduce_sum | solution.py:71
  (4 shorter events, 0.1 us)
Async XLA Ops:
  7.2 1.9 copy-start
  7.2 251.9 %reduce-scatter.2.cloned.1.call-start = ((), (), s32[]{:S(2)}) async-start(), calls=%async_computation.4 | async-start | bytes 12976128 | tf_op jit(solution)/shard_map/reduce_scatter | solution.py:39
  19.9 0.7 copy-start.1
  68.1 194.5 %all-to-all-start = ((bf16[8,40,1536]{2,1,0:T(8,128)(2,1)}), bf16[8,40,1536]{2,1,0:T(8,128)(2,1)}, u32[]{:S(2)}, u32[]{:S(2)}) async-start(bf16[8,40,1536]{2,1,0:T(8,128)(2,1)} %scatter_fusion), calls=%async_computation.1 | async-start | bytes 1966080 | tf_op jit(solution)/shard_map/all_to_all | solution.py:60
  552.4 14.2 %copy-start.2 = (f32[128,2]{0,1:T(2,128)S(1)}, f32[128,2]{0,1:T(2,128)}, u32[]{:S(2)}) copy-start(f32[128,2]{0,1:T(2,128)} %param.15) | copy-start | bytes 3076
  552.4 46.1 %all-to-all-start.2 = ((bf16[8,40,4096]{2,1,0:T(8,128)(2,1)}), bf16[8,40,4096]{2,1,0:T(8,128)(2,1)}, u32[]{:S(2)}, u32[]{:S(2)}) async-start(bf16[8,40,4096]{2,1,0:T(8,128)(2,1)} %bitcast.47), calls=%async_computation.3 | async-start | bytes 5242880 | tf_op jit(solution)/shard_map/all_to_all | solution.py:33
Sparse Core Ops, SparseCore 0:
  20.1 238.9 reduce-scatter.1
